TPU v7x, 256 devices: a whole 4x4x8 slice. The times are simulated.
256 devices in a mesh: pipe: 8 (over z), seq: 32 (over y, x, core).
Axes of the slice: x: 4, y: 4, z: 8, core: 2. Of those that a mesh axis runs over, the one named last changes fastest.
Arguments:
- queries: bfloat16 [8, 4096, 8192], P('pipe', 'seq'), may hold values from -47.6 to 47.6
- keys: bfloat16 [8, 4096, 1024], P('pipe', 'seq'), may hold values from -4 to 4
- values: bfloat16 [8, 4096, 1024], P('pipe', 'seq'), may hold values from -6 to 6
- out_grad: bfloat16 [8, 4096, 8192], P('pipe', 'seq'), may hold values from -6 to 6
- window_blocks: int32 [64, 3], replicated, may hold values from 0 to 63, as said below
- global_blocks: int32 [64, 2], replicated, may hold values from 0 to 63, as said below
- random_blocks: int32 [64, 3], replicated, may hold values from 0 to 63
Outputs:
- handed_queries: bfloat16 [8, 4096, 8192], P('pipe', 'seq')
- handed_keys: bfloat16 [8, 4096, 1024], P('pipe', 'seq')
- handed_values: bfloat16 [8, 4096, 1024], P('pipe', 'seq')
Inputs may be any that keep to these rules, and one draw needn't show every extreme that they name: `window_blocks`: row b lists b - 1, b, b + 1; a neighbour that lies in another document of the pack, or outside the sequence, is replaced by b. `global_blocks`: every row lists the same two blocks: one below 64 // 2, and the last block 64 - 1.
All inputs are finite; a program needn't handle non-finite values.
Results may differ from a plain program's by a relative error of at most 0.012.
The roundings to bfloat16 on the way count: a program that leaves them out, or rounds other values in their place, can miss the bound.
Values may be sent and summed in bfloat16 or wider, within the bound.
No kernel may reach another device: no remote copies, remote signals or barrier semaphores. Data moves between devices by JAX's collectives and lax.ppermute only.
A program may use at most 128 MiB of HBM per device.

v0:
```python
import jax
import jax.numpy as jnp
from jax import lax
from jax.sharding import PartitionSpec as P

HEADS = 64
KV = 8
HD = 128
BLOCK = 64


def from_behind(block, axis, distance):
    devices = range(lax.axis_size(axis))
    route = [(i - distance, i) for i in devices if i - distance in devices]
    return lax.ppermute(block, axis, route)


def block_lists(window_blocks, global_blocks, random_blocks):
    listed = jnp.concatenate([window_blocks, global_blocks, random_blocks], axis=1)
    width = listed.shape[1]
    same = listed[:, :, None] == listed[:, None, :]
    earlier = jnp.arange(width)[None, :] < jnp.arange(width)[:, None]
    repeated = jnp.any(jnp.logical_and(same, earlier[None]), axis=2)
    return (listed, jnp.logical_not(repeated))


def block_grads(q_rows, g_rows, k_blocks, v_blocks, listed, live):
    count = listed.shape[0]
    slots = listed.shape[1]
    block = k_blocks.shape[1]
    depth = k_blocks.shape[2]
    scale = depth ** (-0.5)
    k_near = k_blocks[listed].reshape(count, slots * block, depth)
    v_near = v_blocks[listed].reshape(count, slots * block, depth)
    allowed = jnp.repeat(live, block, axis=1)[:, None, :]
    scores = jnp.einsum("grd,gsd->grs", q_rows, k_near, preferred_element_type=jnp.float32) * scale
    scores = jnp.where(allowed, scores, -jnp.inf)
    top = jnp.max(scores, axis=-1, keepdims=True)
    expd = jnp.exp(scores - top)
    probs = expd / jnp.sum(expd, axis=-1, keepdims=True)
    probs_low = probs.astype(jnp.bfloat16)
    attn_out = jnp.einsum(
        "grs,gsd->grd", probs_low, v_near, preferred_element_type=jnp.float32
    ).astype(jnp.bfloat16)
    attn_out = lax.optimization_barrier(attn_out)
    delta = jnp.sum(
        g_rows.astype(jnp.float32) * attn_out.astype(jnp.float32), axis=-1, keepdims=True
    )
    dprobs = jnp.einsum("grd,gsd->grs", g_rows, v_near, preferred_element_type=jnp.float32)
    ds_low = (probs * (dprobs - delta)).astype(jnp.bfloat16)
    grad_q = (
        jnp.einsum("grs,gsd->grd", ds_low, k_near, preferred_element_type=jnp.float32) * scale
    ).astype(jnp.bfloat16)
    dk_slots = (
        jnp.einsum("grs,grd->gsd", ds_low, q_rows, preferred_element_type=jnp.float32) * scale
    )
    dv_slots = jnp.einsum("grs,grd->gsd", probs_low, g_rows, preferred_element_type=jnp.float32)
    return (
        grad_q,
        dk_slots.reshape(count, slots, block, depth),
        dv_slots.reshape(count, slots, block, depth),
    )


def body(queries, keys, values, out_grad, window_blocks, global_blocks, random_blocks):
    lanes = lax.axis_size("seq")
    tok = queries.shape[1]
    repeat = lanes // KV
    q_local = queries[0].reshape(tok, HEADS, HD)
    g_local = out_grad[0].reshape(tok, HEADS, HD)
    q_heads, g_heads = (
        lax.all_to_all(q_local, "seq", split_axis=1, concat_axis=0, tiled=True),
        lax.all_to_all(g_local, "seq", split_axis=1, concat_axis=0, tiled=True),
    )
    k_all, v_all = (
        lax.all_gather(keys[0], "seq", axis=0, tiled=True),
        lax.all_gather(values[0], "seq", axis=0, tiled=True),
    )
    start = lax.axis_index("seq") // repeat * HD
    k_head = lax.dynamic_slice_in_dim(k_all, start, HD, 1)
    v_head = lax.dynamic_slice_in_dim(v_all, start, HD, 1)
    seqlen = q_heads.shape[0]
    per_device = q_heads.shape[1]
    nblocks = seqlen // BLOCK
    listed, live = block_lists(window_blocks, global_blocks, random_blocks)
    turns = 4
    span = nblocks // turns
    rows = BLOCK * per_device
    q_rows = q_heads.reshape(turns, span, rows, HD)
    g_rows = g_heads.reshape(turns, span, rows, HD)
    k_blocks = k_head.reshape(nblocks, BLOCK, HD)
    v_blocks = v_head.reshape(nblocks, BLOCK, HD)

    def step(carry, parts):
        dk_total, dv_total = carry
        q_part, g_part, list_part, live_part = parts
        grad_q, dk_slots, dv_slots = block_grads(
            q_part, g_part, k_blocks, v_blocks, list_part, live_part
        )
        return (
            (dk_total.at[list_part].add(dk_slots), dv_total.at[list_part].add(dv_slots)),
            grad_q,
        )

    zeros = jnp.zeros((nblocks, BLOCK, HD), jnp.float32)
    inputs = (q_rows, g_rows, listed.reshape(turns, span, -1), live.reshape(turns, span, -1))
    (dk_total, dv_total), grad_q = lax.scan(step, (zeros, zeros), inputs)
    dq_heads = grad_q.reshape(seqlen, per_device, HD)
    dq_tokens = lax.all_to_all(dq_heads, "seq", split_axis=0, concat_axis=1, tiled=True)
    dk_parts, dv_parts = (
        lax.all_to_all(
            dk_total.reshape(seqlen, 1, HD), "seq", split_axis=0, concat_axis=1, tiled=True
        ),
        lax.all_to_all(
            dv_total.reshape(seqlen, 1, HD), "seq", split_axis=0, concat_axis=1, tiled=True
        ),
    )
    dk_tokens = jnp.sum(dk_parts.reshape(tok, KV, repeat, HD), axis=2).astype(jnp.bfloat16)
    dv_tokens = jnp.sum(dv_parts.reshape(tok, KV, repeat, HD), axis=2).astype(jnp.bfloat16)
    dq_flat = dq_tokens.reshape(1, tok, HEADS * HD)
    dk_flat = dk_tokens.reshape(1, tok, KV * HD)
    dv_flat = dv_tokens.reshape(1, tok, KV * HD)
    return from_behind((dq_flat, dk_flat, dv_flat), "pipe", -1)


def solution(mesh):
    in_specs = (
        P("pipe", "seq", None),
        P("pipe", "seq", None),
        P("pipe", "seq", None),
        P("pipe", "seq", None),
        P(),
        P(),
        P(),
    )
    out_specs = (P("pipe", "seq", None), P("pipe", "seq", None), P("pipe", "seq", None))
    return jax.shard_map(body, mesh=mesh, in_specs=in_specs, out_specs=out_specs, check_vma=False)
```

profile of v0, /device:TPU:1, one launch (start us, length us, event | category | flops | bytes accessed | tf_op | source)
XLA Modules:
  0.0 614.2 jit_solution(1255116644743728596)
XLA Ops:
  12.7 8.6 %all-to-all-start = ((bf16[128,64,128]{0,2,1:T(8,128)(2,1)}), bf16[128,64,128]{0,2,1:T(8,128)(2,1)S(1)}, u32[]{:S(2)}, u32[]{:S(2)}) async-start(bf16[128,64,128]{0,2,1:T(8,128)(2,1)} %bitcast.124), calls=%async_computation | async-start | bytes 4194304 | tf_op jit(solution)/shard_map/all_to_all | solution.py:72
  25.4 27.1 %all-to-all-done = bf16[128,64,128]{0,2,1:T(8,128)(2,1)S(1)} async-done(((bf16[128,64,128]{0,2,1:T(8,128)(2,1)}), bf16[128,64,128]{0,2,1:T(8,128)(2,1)S(1)}, u32[]{:S(2)}, u32[]{:S(2)}) %all-to-all-start) | async-done | bytes 2097184 | tf_op jit(solution)/shard_map/all_to_all | solution.py:72
  52.5 6.8 %all-to-all-start.1 = ((bf16[128,64,128]{0,2,1:T(8,128)(2,1)}), bf16[128,64,128]{0,2,1:T(8,128)(2,1)}, u32[]{:S(2)}, u32[]{:S(2)}) async-start(bf16[128,64,128]{0,2,1:T(8,128)(2,1)} %bitcast.123), calls=%async_computation.1 | async-start | bytes 4194304 | tf_op jit(solution)/shard_map/all_to_all | solution.py:73
  63.4 37.7 %all-to-all-done.1 = bf16[128,64,128]{0,2,1:T(8,128)(2,1)} async-done(((bf16[128,64,128]{0,2,1:T(8,128)(2,1)}), bf16[128,64,128]{0,2,1:T(8,128)(2,1)}, u32[]{:S(2)}, u32[]{:S(2)}) %all-to-all-start.1) | async-done | bytes 2097184 | tf_op jit(solution)/shard_map/all_to_all | solution.py:73
  101.0 6.3 %copy.88 = bf16[32,128,2,128]{3,2,1,0:T(2,128)(2,1)} copy(bf16[32,128,2,128]{1,3,2,0:T(8,128)(2,1)} %bitcast.18) | data formatting | bytes 4194304 | tf_op jit(solution)/shard_map/all_to_all | solution.py:73
  108.6 57.6 %all-gather.7.cloned.1.call-done = bf16[1,4096,1024]{2,1,0:T(8,128)(2,1)} async-done(((bf16[1,128,1024]{2,1,0:T(8,128)(2,1)}), bf16[1,4096,1024]{2,1,0:T(8,128)(2,1)}) %all-gather.7.cloned.1.call-update) | async-done | bytes 8388624 | tf_op jit(solution)/shard_map/all_gather | solution.py:77
  171.7 292.9 %while.14 = (s32[]{:T(128)}, f32[64,64,128]{2,1,0:T(8,128)}, f32[64,64,128]{2,1,0:T(8,128)}, bf16[4,16,128,128]{3,2,1,0:T(8,128)(2,1)}, s32[4,16,8]{1,0,2:T(4,12...) while((s32[]{:T(128)}, f32[64,64,128]{2,1,0:T(8,128)}, ...), condition=%wide.region_7.8_spmd, body=%wide.region_1.7_spmd.sunk | while | flops 1628176256 | bytes 138499472 | solution.py:107
  172.9 4.1 fusion.63
  177.2 4.9 fusion.64
  193.0 4.2 convolution_multiply_fusion.3
  197.2 20.0 %scatter_fusion = f32[64,64,128]{2,1,0:T(8,128)} fusion(f32[64,64,128]{2,1,0:T(8,128)} %get-tuple-element.221, s32[128]{0:T(128)S(1)} %reshape.204, f32[128,64,128]{2,1,0:T(8,128)} %bitcast.110), kind=kCustom, calls=%fused_computation.2.clone.1 | custom fusion | flops 1048576 | bytes 12583424 | tf_op jit(solution)/shard_map/while/body/eval_jaxpr/scatter-add | solution.py:101
  224.7 20.3 %scatter_fusion.1 = f32[64,64,128]{2,1,0:T(8,128)} fusion(f32[64,64,128]{2,1,0:T(8,128)} %get-tuple-element.222, s32[128]{0:T(128)S(1)} %reshape.204, f32[128,64,128]{2,1,0:T(8,128)} %bitcast.109), kind=kCustom, calls=%fused_computation.3.clone.1 | custom fusion | flops 1048576 | bytes 12583424 | tf_op jit(solution)/shard_map/while/body/eval_jaxpr/scatter-add | solution.py:101
  246.1 4.1 fusion.63
  250.5 4.9 fusion.64
  266.3 4.2 convolution_multiply_fusion.3
  270.5 20.0 %scatter_fusion = f32[64,64,128]{2,1,0:T(8,128)} fusion(f32[64,64,128]{2,1,0:T(8,128)} %get-tuple-element.221, s32[128]{0:T(128)S(1)} %reshape.204, f32[128,64,128]{2,1,0:T(8,128)} %bitcast.110), kind=kCustom, calls=%fused_computation.2.clone.1 | custom fusion | flops 1048576 | bytes 12583424 | tf_op jit(solution)/shard_map/while/body/eval_jaxpr/scatter-add | solution.py:101
  298.0 20.1 %scatter_fusion.1 = f32[64,64,128]{2,1,0:T(8,128)} fusion(f32[64,64,128]{2,1,0:T(8,128)} %get-tuple-element.222, s32[128]{0:T(128)S(1)} %reshape.204, f32[128,64,128]{2,1,0:T(8,128)} %bitcast.109), kind=kCustom, calls=%fused_computation.3.clone.1 | custom fusion | flops 1048576 | bytes 12583424 | tf_op jit(solution)/shard_map/while/body/eval_jaxpr/scatter-add | solution.py:101
  319.3 4.1 fusion.63
  323.7 4.9 fusion.64
  339.5 4.2 convolution_multiply_fusion.3
  343.7 20.0 %scatter_fusion = f32[64,64,128]{2,1,0:T(8,128)} fusion(f32[64,64,128]{2,1,0:T(8,128)} %get-tuple-element.221, s32[128]{0:T(128)S(1)} %reshape.204, f32[128,64,128]{2,1,0:T(8,128)} %bitcast.110), kind=kCustom, calls=%fused_computation.2.clone.1 | custom fusion | flops 1048576 | bytes 12583424 | tf_op jit(solution)/shard_map/while/body/eval_jaxpr/scatter-add | solution.py:101
  371.2 20.2 %scatter_fusion.1 = f32[64,64,128]{2,1,0:T(8,128)} fusion(f32[64,64,128]{2,1,0:T(8,128)} %get-tuple-element.222, s32[128]{0:T(128)S(1)} %reshape.204, f32[128,64,128]{2,1,0:T(8,128)} %bitcast.109), kind=kCustom, calls=%fused_computation.3.clone.1 | custom fusion | flops 1048576 | bytes 12583424 | tf_op jit(solution)/shard_map/while/body/eval_jaxpr/scatter-add | solution.py:101
  392.5 4.1 fusion.63
  396.9 4.9 fusion.64
  412.7 4.2 convolution_multiply_fusion.3
  416.9 20.0 %scatter_fusion = f32[64,64,128]{2,1,0:T(8,128)} fusion(f32[64,64,128]{2,1,0:T(8,128)} %get-tuple-element.221, s32[128]{0:T(128)S(1)} %reshape.204, f32[128,64,128]{2,1,0:T(8,128)} %bitcast.110), kind=kCustom, calls=%fused_computation.2.clone.1 | custom fusion | flops 1048576 | bytes 12583424 | tf_op jit(solution)/shard_map/while/body/eval_jaxpr/scatter-add | solution.py:101
  444.4 20.2 %scatter_fusion.1 = f32[64,64,128]{2,1,0:T(8,128)} fusion(f32[64,64,128]{2,1,0:T(8,128)} %get-tuple-element.222, s32[128]{0:T(128)S(1)} %reshape.204, f32[128,64,128]{2,1,0:T(8,128)} %bitcast.109), kind=kCustom, calls=%fused_computation.3.clone.1 | custom fusion | flops 1048576 | bytes 12583424 | tf_op jit(solution)/shard_map/while/body/eval_jaxpr/scatter-add | solution.py:101
  464.6 34.0 %all_to_all.75 = bf16[4096,2,128]{2,1,0:T(2,128)(2,1)} all-to-all(bf16[4096,2,128]{2,1,0:T(2,128)(2,1)} %bitcast.126), channel_id=1, replica_groups=mesh['pipe'=8,'seq'=32] {'seq'}, dimensions={0} | all-to-all | bytes 4194304 | tf_op jit(solution)/shard_map/all_to_all | solution.py:109
  498.6 32.3 %all_to_all.76 = f32[4096,1,128]{2,1,0:T(1,128)} all-to-all(f32[4096,1,128]{2,1,0:T(1,128)S(1)} %bitcast.111), channel_id=1, replica_groups=mesh['pipe'=8,'seq'=32] {'seq'}, dimensions={0} | all-to-all | bytes 4194304 | tf_op jit(solution)/shard_map/all_to_all | solution.py:111
  546.8 16.5 %all-to-all-done.4 = f32[4096,1,128]{2,1,0:T(1,128)S(1)} async-done(((f32[4096,1,128]{2,1,0:T(1,128)}), f32[4096,1,128]{2,1,0:T(1,128)S(1)}, u32[]{:S(2)}, u32[]{:S(2)}) %all-to-all-start.4) | async-done | bytes 2097184 | tf_op jit(solution)/shard_map/all_to_all | solution.py:114
  564.9 31.9 %collective-permute-done.1 = bf16[1,128,1024]{1,2,0:T(8,128)(2,1)S(1)} collective-permute-done((bf16[1,128,1024]{1,2,0:T(8,128)(2,1)S(1)}, bf16[1,128,1024]{1,2,0:T(8,128)(2,1)S(1)}, u32[]{:S(2)}, u32[]{:S(2)}) %collective-permute-start.1) | collective-permute-done | bytes 262176 | tf_op jit(solution)/shard_map/ppermute | solution.py:15
  597.7 4.8 collective-permute-done.2
  (150 shorter events, 122.6 us)
Async XLA Ops:
  7.2 100.2 %all-gather.5.cloned.1.call-start = ((), (), s32[]{:S(2)}) async-start(), calls=%async_computation.5 | async-start | bytes 8650752 | tf_op jit(solution)/shard_map/all_gather | solution.py:76
  7.9 158.3 %all-gather.7.cloned.1.call-start = ((), (), s32[]{:S(2)}) async-start(), calls=%async_computation.6 | async-start | bytes 8650752 | tf_op jit(solution)/shard_map/all_gather | solution.py:77
  12.7 39.8 %all-to-all-start = ((bf16[128,64,128]{0,2,1:T(8,128)(2,1)}), bf16[128,64,128]{0,2,1:T(8,128)(2,1)S(1)}, u32[]{:S(2)}, u32[]{:S(2)}) async-start(bf16[128,64,128]{0,2,1:T(8,128)(2,1)} %bitcast.124), calls=%async_computation | async-start | bytes 4194304 | tf_op jit(solution)/shard_map/all_to_all | solution.py:72
  52.5 6.8 %copy-start.6 = (s32[64,3]{0,1:T(4,128)S(1)}, s32[64,3]{0,1:T(4,128)}, u32[]{:S(2)}) copy-start(s32[64,3]{0,1:T(4,128)} %param.15) | copy-start | bytes 2308
  52.5 6.8 %copy-start.7 = (s32[64,3]{0,1:T(4,128)S(1)}, s32[64,3]{0,1:T(4,128)}, u32[]{:S(2)}) copy-start(s32[64,3]{0,1:T(4,128)} %param.13) | copy-start | bytes 2308
  52.5 6.8 %copy-start.8 = (s32[64,2]{0,1:T(2,128)S(1)}, s32[64,2]{0,1:T(2,128)}, u32[]{:S(2)}) copy-start(s32[64,2]{0,1:T(2,128)} %param.14) | copy-start | bytes 1540
  52.5 48.6 %all-to-all-start.1 = ((bf16[128,64,128]{0,2,1:T(8,128)(2,1)}), bf16[128,64,128]{0,2,1:T(8,128)(2,1)}, u32[]{:S(2)}, u32[]{:S(2)}) async-start(bf16[128,64,128]{0,2,1:T(8,128)(2,1)} %bitcast.123), calls=%async_computation.1 | async-start | bytes 4194304 | tf_op jit(solution)/shard_map/all_to_all | solution.py:73
  172.9 4.1 copy-start.1
  182.1 1.9 copy-start.3
  187.5 2.4 copy-start.5
  187.5 2.9 copy-start.2
  193.0 4.2 copy-start.4
  246.1 4.1 copy-start.1
  255.4 1.9 copy-start.3
  260.7 2.4 copy-start.5
  260.7 2.9 copy-start.2
  266.3 4.2 copy-start.4
  319.3 4.1 copy-start.1
  328.6 1.9 copy-start.3
  333.9 2.4 copy-start.5
  333.9 2.9 copy-start.2
  339.5 4.2 copy-start.4
  392.5 4.1 copy-start.1
  401.8 1.9 copy-start.3
  407.1 2.4 copy-start.5
  407.1 2.9 copy-start.2
  412.7 4.2 copy-start.4
  464.6 34.0 %copy-start = (f32[64,64,128]{2,1,0:T(8,128)S(1)}, f32[64,64,128]{2,1,0:T(8,128)}, u32[]{:S(2)}) copy-start(f32[64,64,128]{2,1,0:T(8,128)} %get-tuple-element.58) | copy-start | bytes 6291460
  530.9 32.4 %all-to-all-start.4 = ((f32[4096,1,128]{2,1,0:T(1,128)}), f32[4096,1,128]{2,1,0:T(1,128)S(1)}, u32[]{:S(2)}, u32[]{:S(2)}) async-start(f32[4096,1,128]{2,1,0:T(1,128)} %bitcast.30), calls=%async_computation.4 | async-start | bytes 4194304 | tf_op jit(solution)/shard_map/all_to_all | solution.py:114
  542.3 61.0 %collective-permute-start = (bf16[1,128,8192]{1,2,0:T(8,128)(2,1)}, bf16[1,128,8192]{1,2,0:T(8,128)(2,1)}, u32[]{:S(2)}, u32[]{:S(2)}) collective-permute-start(bf16[1,128,8192]{1,2,0:T(8,128)(2,1)} %bitcast.127), channel_id=1, source_target_pairs={{32,0},{64,32},{96,64},{128,96},{160,128},{192,160},{224,192},{33,... | collective-permute-start | bytes 6291464 | tf_op jit(solution)/shard_map/ppermute | solution.py:15
  545.5 51.3 %collective-permute-start.1 = (bf16[1,128,1024]{1,2,0:T(8,128)(2,1)S(1)}, bf16[1,128,1024]{1,2,0:T(8,128)(2,1)S(1)}, u32[]{:S(2)}, u32[]{:S(2)}) collective-permute-start(bf16[1,128,1024]{1,2,0:T(8,128)(2,1)S(1)} %bitcast.129), channel_id=1, source_target_pairs={{32,0},{64,32},{96,64},{128,96},{160,128},{192,160},{224,192},{33,... | collective-permute-start | bytes 786440 | tf_op jit(solution)/shard_map/ppermute | solution.py:15
  563.6 38.8 %collective-permute-start.2 = (bf16[1,128,1024]{1,2,0:T(8,128)(2,1)S(1)}, bf16[1,128,1024]{1,2,0:T(8,128)(2,1)S(1)}, u32[]{:S(2)}, u32[]{:S(2)}) collective-permute-start(bf16[1,128,1024]{1,2,0:T(8,128)(2,1)S(1)} %bitcast.130), channel_id=1, source_target_pairs={{32,0},{64,32},{96,64},{128,96},{160,128},{192,160},{224,192},{33,... | collective-permute-start | bytes 786440 | tf_op jit(solution)/shard_map/ppermute | solution.py:15
Sparse Core Ops, SparseCore 0:
  10.5 93.9 all-gather.4
  107.1 59.0 all-gather.6
where the time goes:
time: 618 us; the launch traced here: 614 us
  other arithmetic  185 us (30%)
  waiting for transfers between devices  177 us (29%)
  matrix products  83.6 us (14%)
  blocking collectives  66.3 us (11%)
  local copies, waits for them, and re-layouts  64 us (10%)
  starting transfers between devices  23.3 us (4%)
  between operations  14.2 us (2%)
    scatter-add x4, other arithmetic, step(): dv_total.at[list_part].add(dv_slots)  80.8 us
    scatter-add x4, other arithmetic, step(): dk_total.at[list_part].add(dk_slots)  80.1 us
    all_gather x1, waiting for transfers between devices, body(): lax.all_gather(values[0], 'seq', axis=0, tiled=True)  57.6 us
    all_to_all x1, waiting for transfers between devices, body(): lax.all_to_all(g_local, 'seq', split_axis=1, concat_axis=0, tiled=True)  37.7 us
    ppermute x3, waiting for transfers between devices, from_behind(): return lax.ppermute(block, axis, route)  36.7 us
    all_to_all x1, blocking collectives, body(): lax.all_to_all(dq_heads, 'seq', split_axis=0, concat_axis=1, tiled=True)  34 us
    all_to_all x1, blocking collectives, body(): lax.all_to_all(dk_total.reshape(seqlen, 1, HD), 'seq', split_axis=0, conc...  32.3 us
    all_to_all x1, waiting for transfers between devices, body(): lax.all_to_all(q_local, 'seq', split_axis=1, concat_axis=0, tiled=True)  27.1 us
  transfers between devices with their start and end apart: 8, of which 6 were waited for; matrix products, arithmetic and copies ran while one was open for 5% of the time, Pallas kernels for 0%

commit v1 on v0

--- a/solution.py
+++ b/solution.py
@@ -74,7 +74,9 @@
     )
     k_all, v_all = (
         lax.all_gather(keys[0], "seq", axis=0, tiled=True),
-        lax.all_gather(values[0], "seq", axis=0, tiled=True),
+        jnp.concatenate(
+            lax.all_to_all(jnp.stack([values[0]] * lax.axis_size("seq")), "seq", 0, 0), axis=0
+        ),
     )
     start = lax.axis_index("seq") // repeat * HD
     k_head = lax.dynamic_slice_in_dim(k_all, start, HD, 1)

time: 618 us -> 673 us (1.089)
  blocking collectives: 66.3 us -> 121 us
    all_gather x1 -> x0, waiting for transfers between devices: 57.6 us -> none  [body(): lax.all_gather(values[0], 'seq', axis=0, tiled=True)]
    all_to_all x1, waiting for transfers between devices: 37.7 us -> 90 us  [body(): lax.all_to_all(jnp.stack([values[0]] * lax.axis_size('seq')), 'seq', 0, 0)]
    all_to_all x0 -> x1, blocking collectives: none -> 50.1 us  [body(): lax.all_to_all(g_local, 'seq', split_axis=1, concat_axis=0, tiled=True)]
    unnamed x13 -> x15, local copies, waits for them, and re-layouts: 13.9 us -> 13.9 us
  transfers between devices with their start and end apart: 8 -> 7, of which waited for: 6 -> 5; matrix products, arithmetic and copies ran while one was open for 5% -> 5% of each run, Pallas kernels for 0% -> 0%
where the time goes in v1:
time: 673 us; the launch traced here: 668 us
  other arithmetic  186 us (28%)
  waiting for transfers between devices  173 us (26%)
  blocking collectives  121 us (18%)
  matrix products  83.6 us (12%)
  local copies, waits for them, and re-layouts  68.3 us (10%)
  starting transfers between devices  22.2 us (3%)
  between operations  14.2 us (2%)
    all_to_all x1, waiting for transfers between devices, body(): lax.all_to_all(jnp.stack([values[0]] * lax.axis_size('seq')), 'seq', 0, 0)  90 us
    scatter-add x4, other arithmetic, step(): dv_total.at[list_part].add(dv_slots)  81 us
    scatter-add x4, other arithmetic, step(): dk_total.at[list_part].add(dk_slots)  80.1 us
    all_to_all x1, blocking collectives, body(): lax.all_to_all(g_local, 'seq', split_axis=1, concat_axis=0, tiled=True)  50.1 us
    all_to_all x1, blocking collectives, body(): lax.all_to_all(dq_heads, 'seq', split_axis=0, concat_axis=1, tiled=True)  38.6 us
    ppermute x3, waiting for transfers between devices, from_behind(): return lax.ppermute(block, axis, route)  38.2 us
    all_to_all x1, blocking collectives, body(): lax.all_to_all(dk_total.reshape(seqlen, 1, HD), 'seq', split_axis=0, conc...  32.1 us
    all_to_all x1, waiting for transfers between devices, body(): lax.all_to_all(q_local, 'seq', split_axis=1, concat_axis=0, tiled=True)  27.1 us
  transfers between devices with their start and end apart: 7, of which 5 were waited for; matrix products, arithmetic and copies ran while one was open for 5% of the time, Pallas kernels for 0%

profile of v1, /device:TPU:1, one launch (start us, length us, event | category | flops | bytes accessed | tf_op | source)
XLA Modules:
  0.0 667.9 jit_solution(11795916260994194285)
XLA Ops:
  12.0 8.6 %all-to-all-start = ((bf16[128,64,128]{0,2,1:T(8,128)(2,1)}), bf16[128,64,128]{0,2,1:T(8,128)(2,1)S(1)}, u32[]{:S(2)}, u32[]{:S(2)}) async-start(bf16[128,64,128]{0,2,1:T(8,128)(2,1)} %bitcast.126), calls=%async_computation | async-start | bytes 4194304 | tf_op jit(solution)/shard_map/all_to_all | solution.py:72
  24.6 27.1 %all-to-all-done = bf16[128,64,128]{0,2,1:T(8,128)(2,1)S(1)} async-done(((bf16[128,64,128]{0,2,1:T(8,128)(2,1)}), bf16[128,64,128]{0,2,1:T(8,128)(2,1)S(1)}, u32[]{:S(2)}, u32[]{:S(2)}) %all-to-all-start) | async-done | bytes 2097184 | tf_op jit(solution)/shard_map/all_to_all | solution.py:72
  51.8 50.1 %all_to_all.80 = bf16[128,64,128]{0,2,1:T(8,128)(2,1)} all-to-all(bf16[128,64,128]{0,2,1:T(8,128)(2,1)} %bitcast.127), channel_id=1, replica_groups=mesh['pipe'=8,'seq'=32] {'seq'}, dimensions={1} | all-to-all | bytes 4194304 | tf_op jit(solution)/shard_map/all_to_all | solution.py:73
  101.9 4.3 stack.3
  106.2 5.7 all-to-all-start.2
  116.1 6.2 copy.88
  122.3 90.0 %all-to-all-done.2 = bf16[32,128,1024]{2,1,0:T(8,128)(2,1)} async-done(((bf16[32,128,1024]{2,1,0:T(8,128)(2,1)}), bf16[32,128,1024]{2,1,0:T(8,128)(2,1)}, u32[]{:S(2)}, u32[]{:S(2)}) %all-to-all-start.2) | async-done | bytes 8388640 | tf_op jit(solution)/shard_map/all_to_all | solution.py:78
  219.2 293.2 %while.14 = (s32[]{:T(128)}, f32[64,64,128]{2,1,0:T(8,128)}, f32[64,64,128]{2,1,0:T(8,128)}, bf16[4,16,128,128]{3,2,1,0:T(8,128)(2,1)}, s32[4,16,8]{1,0,2:T(4,12...) while((s32[]{:T(128)}, f32[64,64,128]{2,1,0:T(8,128)}, ...), condition=%wide.region_7.8_spmd, body=%wide.region_1.7_spmd.sunk | while | flops 1628176256 | bytes 138499472 | solution.py:109
  225.9 4.9 fusion.64
  240.5 4.2 convolution_multiply_fusion.3
  244.7 20.0 %scatter_fusion = f32[64,64,128]{2,1,0:T(8,128)} fusion(f32[64,64,128]{2,1,0:T(8,128)} %get-tuple-element.221, s32[128]{0:T(128)S(1)} %reshape.206, f32[128,64,128]{2,1,0:T(8,128)} %bitcast.112), kind=kCustom, calls=%fused_computation.2.clone.1 | custom fusion | flops 1048576 | bytes 12583424 | tf_op jit(solution)/shard_map/while/body/eval_jaxpr/scatter-add | solution.py:103
  272.2 20.3 %scatter_fusion.1 = f32[64,64,128]{2,1,0:T(8,128)} fusion(f32[64,64,128]{2,1,0:T(8,128)} %get-tuple-element.222, s32[128]{0:T(128)S(1)} %reshape.206, f32[128,64,128]{2,1,0:T(8,128)} %bitcast.111), kind=kCustom, calls=%fused_computation.3.clone.1 | custom fusion | flops 1048576 | bytes 12583424 | tf_op jit(solution)/shard_map/while/body/eval_jaxpr/scatter-add | solution.py:103
  294.9 4.1 fusion.63
  299.3 4.9 fusion.64
  313.8 4.2 convolution_multiply_fusion.3
  318.0 20.0 %scatter_fusion = f32[64,64,128]{2,1,0:T(8,128)} fusion(f32[64,64,128]{2,1,0:T(8,128)} %get-tuple-element.221, s32[128]{0:T(128)S(1)} %reshape.206, f32[128,64,128]{2,1,0:T(8,128)} %bitcast.112), kind=kCustom, calls=%fused_computation.2.clone.1 | custom fusion | flops 1048576 | bytes 12583424 | tf_op jit(solution)/shard_map/while/body/eval_jaxpr/scatter-add | solution.py:103
  345.6 20.4 %scatter_fusion.1 = f32[64,64,128]{2,1,0:T(8,128)} fusion(f32[64,64,128]{2,1,0:T(8,128)} %get-tuple-element.222, s32[128]{0:T(128)S(1)} %reshape.206, f32[128,64,128]{2,1,0:T(8,128)} %bitcast.111), kind=kCustom, calls=%fused_computation.3.clone.1 | custom fusion | flops 1048576 | bytes 12583424 | tf_op jit(solution)/shard_map/while/body/eval_jaxpr/scatter-add | solution.py:103
  368.3 4.1 fusion.63
  372.7 4.9 fusion.64
  387.3 4.2 convolution_multiply_fusion.3
  391.5 20.0 %scatter_fusion = f32[64,64,128]{2,1,0:T(8,128)} fusion(f32[64,64,128]{2,1,0:T(8,128)} %get-tuple-element.221, s32[128]{0:T(128)S(1)} %reshape.206, f32[128,64,128]{2,1,0:T(8,128)} %bitcast.112), kind=kCustom, calls=%fused_computation.2.clone.1 | custom fusion | flops 1048576 | bytes 12583424 | tf_op jit(solution)/shard_map/while/body/eval_jaxpr/scatter-add | solution.py:103
  419.0 20.2 %scatter_fusion.1 = f32[64,64,128]{2,1,0:T(8,128)} fusion(f32[64,64,128]{2,1,0:T(8,128)} %get-tuple-element.222, s32[128]{0:T(128)S(1)} %reshape.206, f32[128,64,128]{2,1,0:T(8,128)} %bitcast.111), kind=kCustom, calls=%fused_computation.3.clone.1 | custom fusion | flops 1048576 | bytes 12583424 | tf_op jit(solution)/shard_map/while/body/eval_jaxpr/scatter-add | solution.py:103
  441.5 4.1 fusion.63
  445.9 4.9 fusion.64
  460.5 4.2 convolution_multiply_fusion.3
  464.7 20.0 %scatter_fusion = f32[64,64,128]{2,1,0:T(8,128)} fusion(f32[64,64,128]{2,1,0:T(8,128)} %get-tuple-element.221, s32[128]{0:T(128)S(1)} %reshape.206, f32[128,64,128]{2,1,0:T(8,128)} %bitcast.112), kind=kCustom, calls=%fused_computation.2.clone.1 | custom fusion | flops 1048576 | bytes 12583424 | tf_op jit(solution)/shard_map/while/body/eval_jaxpr/scatter-add | solution.py:103
  492.2 20.2 %scatter_fusion.1 = f32[64,64,128]{2,1,0:T(8,128)} fusion(f32[64,64,128]{2,1,0:T(8,128)} %get-tuple-element.222, s32[128]{0:T(128)S(1)} %reshape.206, f32[128,64,128]{2,1,0:T(8,128)} %bitcast.111), kind=kCustom, calls=%fused_computation.3.clone.1 | custom fusion | flops 1048576 | bytes 12583424 | tf_op jit(solution)/shard_map/while/body/eval_jaxpr/scatter-add | solution.py:103
  512.4 38.6 %all_to_all.81 = bf16[4096,2,128]{2,1,0:T(2,128)(2,1)} all-to-all(bf16[4096,2,128]{2,1,0:T(2,128)(2,1)} %bitcast.129), channel_id=1, replica_groups=mesh['pipe'=8,'seq'=32] {'seq'}, dimensions={0} | all-to-all | bytes 4194304 | tf_op jit(solution)/shard_map/all_to_all | solution.py:111
  551.0 32.1 %all_to_all.82 = f32[4096,1,128]{2,1,0:T(1,128)} all-to-all(f32[4096,1,128]{2,1,0:T(1,128)S(1)} %bitcast.113), channel_id=1, replica_groups=mesh['pipe'=8,'seq'=32] {'seq'}, dimensions={0} | all-to-all | bytes 4194304 | tf_op jit(solution)/shard_map/all_to_all | solution.py:113
  599.0 16.5 %all-to-all-done.5 = f32[4096,1,128]{2,1,0:T(1,128)S(1)} async-done(((f32[4096,1,128]{2,1,0:T(1,128)}), f32[4096,1,128]{2,1,0:T(1,128)S(1)}, u32[]{:S(2)}, u32[]{:S(2)}) %all-to-all-start.5) | async-done | bytes 2097184 | tf_op jit(solution)/shard_map/all_to_all | solution.py:116
  617.1 33.4 %collective-permute-done.1 = bf16[1,128,1024]{1,2,0:T(8,128)(2,1)S(1)} collective-permute-done((bf16[1,128,1024]{1,2,0:T(8,128)(2,1)S(1)}, bf16[1,128,1024]{1,2,0:T(8,128)(2,1)S(1)}, u32[]{:S(2)}, u32[]{:S(2)}) %collective-permute-start.1) | collective-permute-done | bytes 262176 | tf_op jit(solution)/shard_map/ppermute | solution.py:15
  651.4 4.8 collective-permute-done.2
  (151 shorter events, 126.1 us)
Async XLA Ops:
  7.2 206.5 %all-gather.3.cloned.1.call-start = ((), (), s32[]{:S(2)}) async-start(), calls=%async_computation.6 | async-start | bytes 8650752 | tf_op jit(solution)/shard_map/all_gather | solution.py:76
  12.0 39.8 %all-to-all-start = ((bf16[128,64,128]{0,2,1:T(8,128)(2,1)}), bf16[128,64,128]{0,2,1:T(8,128)(2,1)S(1)}, u32[]{:S(2)}, u32[]{:S(2)}) async-start(bf16[128,64,128]{0,2,1:T(8,128)(2,1)} %bitcast.126), calls=%async_computation | async-start | bytes 4194304 | tf_op jit(solution)/shard_map/all_to_all | solution.py:72
  51.8 50.1 %copy-start.6 = (bf16[1,128,1024]{2,1,0:T(8,128)(2,1)S(1)}, bf16[1,128,1024]{2,1,0:T(8,128)(2,1)}, u32[]{:S(2)}) copy-start(bf16[1,128,1024]{2,1,0:T(8,128)(2,1)} %param.11) | copy-start | bytes 786436
  106.2 5.8 copy-start.7
  106.2 5.8 copy-start.8
  106.2 5.8 copy-start.9
  106.2 106.2 %all-to-all-start.2 = ((bf16[32,128,1024]{2,1,0:T(8,128)(2,1)}), bf16[32,128,1024]{2,1,0:T(8,128)(2,1)}, u32[]{:S(2)}, u32[]{:S(2)}) async-start(bf16[32,128,1024]{2,1,0:T(8,128)(2,1)} %stack.3), calls=%async_computation.2 | async-start | bytes 16777216 | tf_op jit(solution)/shard_map/all_to_all | solution.py:78
  221.6 4.1 copy-start.1
  230.8 1.9 copy-start.3
  234.9 2.4 copy-start.5
  234.9 2.9 copy-start.2
  240.5 4.2 copy-start.4
  294.9 4.1 copy-start.1
  304.2 1.9 copy-start.3
  308.3 2.4 copy-start.5
  308.3 2.9 copy-start.2
  313.8 4.2 copy-start.4
  368.3 4.1 copy-start.1
  377.6 1.9 copy-start.3
  381.7 2.4 copy-start.5
  381.7 2.9 copy-start.2
  387.3 4.2 copy-start.4
  441.5 4.1 copy-start.1
  450.8 1.9 copy-start.3
  454.9 2.4 copy-start.5
  454.9 2.9 copy-start.2
  460.5 4.2 copy-start.4
  512.4 38.6 %copy-start = (f32[64,64,128]{2,1,0:T(8,128)S(1)}, f32[64,64,128]{2,1,0:T(8,128)}, u32[]{:S(2)}) copy-start(f32[64,64,128]{2,1,0:T(8,128)} %get-tuple-element.58) | copy-start | bytes 6291460
  583.1 32.4 %all-to-all-start.5 = ((f32[4096,1,128]{2,1,0:T(1,128)}), f32[4096,1,128]{2,1,0:T(1,128)S(1)}, u32[]{:S(2)}, u32[]{:S(2)}) async-start(f32[4096,1,128]{2,1,0:T(1,128)} %bitcast.32), calls=%async_computation.5 | async-start | bytes 4194304 | tf_op jit(solution)/shard_map/all_to_all | solution.py:116
  594.5 62.5 %collective-permute-start = (bf16[1,128,8192]{1,2,0:T(8,128)(2,1)}, bf16[1,128,8192]{1,2,0:T(8,128)(2,1)}, u32[]{:S(2)}, u32[]{:S(2)}) collective-permute-start(bf16[1,128,8192]{1,2,0:T(8,128)(2,1)} %bitcast.130), channel_id=1, source_target_pairs={{32,0},{64,32},{96,64},{128,96},{160,128},{192,160},{224,192},{33,... | collective-permute-start | bytes 6291464 | tf_op jit(solution)/shard_map/ppermute | solution.py:15
  597.7 52.8 %collective-permute-start.1 = (bf16[1,128,1024]{1,2,0:T(8,128)(2,1)S(1)}, bf16[1,128,1024]{1,2,0:T(8,128)(2,1)S(1)}, u32[]{:S(2)}, u32[]{:S(2)}) collective-permute-start(bf16[1,128,1024]{1,2,0:T(8,128)(2,1)S(1)} %bitcast.133), channel_id=1, source_target_pairs={{32,0},{64,32},{96,64},{128,96},{160,128},{192,160},{224,192},{33,... | collective-permute-start | bytes 786440 | tf_op jit(solution)/shard_map/ppermute | solution.py:15
  615.8 40.3 %collective-permute-start.2 = (bf16[1,128,1024]{1,2,0:T(8,128)(2,1)S(1)}, bf16[1,128,1024]{1,2,0:T(8,128)(2,1)S(1)}, u32[]{:S(2)}, u32[]{:S(2)}) collective-permute-start(bf16[1,128,1024]{1,2,0:T(8,128)(2,1)S(1)} %bitcast.134), channel_id=1, source_target_pairs={{32,0},{64,32},{96,64},{128,96},{160,128},{192,160},{224,192},{33,... | collective-permute-start | bytes 786440 | tf_op jit(solution)/shard_map/ppermute | solution.py:15
Sparse Core Ops, SparseCore 0:
  10.5 92.8 all-gather.2
